TPU v7x, 512 devices: a whole 4x8x8 slice. The times are simulated.
512 devices in a mesh: region: 8 (over z), sub: 64 (over y, x, core).
Axes of the slice: x: 4, y: 8, z: 8, core: 2. Of those that a mesh axis runs over, the one named last changes fastest.
Arguments:
- right_side: bfloat16 [8, 64, 1024, 256], P('region', 'sub'), may hold values from -6 to 6
- local_inverse: bfloat16 [8, 64, 1024, 1024], P('region', 'sub')
- coupling: bfloat16 [8, 64, 4, 256, 256], P('region', 'sub'), may hold values from -0.75 to 0.75
- margin_blocks: int32 [4, 8, 64, 2], P(None, 'region', 'sub'), may hold values from 0 to 7, as said below
- partner: int32 [4, 512], replicated, may hold values from 0 to 511, as said below
- restriction: bfloat16 [8, 64, 64, 1024], P('region', 'sub'), may hold values from -0.375 to 0.375
- coarse_rows: bfloat16 [8, 4096, 4096], P('region', 'sub')
Outputs:
- solution: bfloat16 [8, 64, 1024, 256], P('region', 'sub')
Inputs may be any that keep to these rules, and one draw needn't show every extreme that they name: `margin_blocks`: for each colour, subdomain and k, a block number below 8; the 2 numbers of one colour and subdomain are distinct. For each colour a perfect matching of all subdomains: the partner of a subdomain's partner is the subdomain itself, and no subdomain is its own partner.
All inputs are finite; a program needn't handle non-finite values.
Results may differ from a plain program's by a relative error of at most 0.0052.
Values may be sent and summed in bfloat16 or wider, within the bound.
No kernel may reach another device: no remote copies, remote signals or barrier semaphores. Data moves between devices by JAX's collectives and lax.ppermute only.
A program may use at most 64 MiB of HBM per device.

v0:
```python
import jax
import jax.numpy as jnp
from jax import lax
from jax.sharding import PartitionSpec as P

BLK = 128
OVL_BLK = 2
COLORS = 4


def shards(right_side, local_inverse, coupling, margin_blocks, partner, restriction, coarse_rows):
    inverse = local_inverse[0, 0]
    tile_set = coupling[0, 0]
    own_blocks = margin_blocks[:, 0, 0, :]
    row_count = inverse.shape[0]
    columns = right_side.shape[-1]
    block_count = row_count // BLK
    span_rows = tile_set.shape[-1]
    sub_peers = lax.axis_size("sub")
    region_peers = lax.axis_size("region")
    all_peers = sub_peers * region_peers
    piece_len = span_rows * columns // all_peers
    residual = right_side[0, 0].astype(jnp.float32)
    accumulated = jnp.zeros(residual.shape, jnp.float32)
    block_ids = jnp.arange(block_count, dtype=jnp.int32)
    for colour in range(COLORS):
        picked = own_blocks[colour]
        tiled = residual.reshape(block_count, BLK, columns)
        sent_rows = jnp.take(tiled, picked, axis=0).reshape(span_rows, columns).astype(jnp.bfloat16)
        pieces = sent_rows.reshape(region_peers, sub_peers, piece_len)
        relayed = lax.all_to_all(
            lax.all_to_all(pieces, "region", split_axis=0, concat_axis=0, tiled=True),
            "sub",
            split_axis=1,
            concat_axis=1,
            tiled=True,
        )
        relayed = jnp.take(relayed.reshape(all_peers, piece_len), partner[colour], axis=0)
        returned = lax.all_to_all(
            lax.all_to_all(
                relayed.reshape(region_peers, sub_peers, piece_len),
                "region",
                split_axis=0,
                concat_axis=0,
                tiled=True,
            ),
            "sub",
            split_axis=1,
            concat_axis=1,
            tiled=True,
        )
        received = returned.reshape(span_rows, columns)
        coupled = jnp.dot(tile_set[colour], received, preferred_element_type=jnp.float32)
        one_hot = (picked[:, None] == block_ids[None, :]).astype(jnp.float32)
        added = jnp.einsum(
            "kb,kin->bin",
            one_hot,
            coupled.reshape(OVL_BLK, BLK, columns),
            precision=lax.Precision.HIGHEST,
        )
        widened = residual + added.reshape(row_count, columns)
        shaped = widened.astype(jnp.bfloat16)
        correction = jnp.dot(inverse, shaped, preferred_element_type=jnp.float32)
        accumulated = accumulated + correction
        residual = widened - 0.25 * correction
    settled = residual.astype(jnp.bfloat16)
    own_restriction = restriction[0, 0]
    projected = jnp.dot(own_restriction, settled, preferred_element_type=jnp.float32).astype(
        jnp.bfloat16
    )
    own_rows = coarse_rows[0]
    coarse = jnp.dot(
        own_rows,
        lax.all_gather(projected, "sub", axis=0, tiled=True),
        preferred_element_type=jnp.float32,
    ).astype(jnp.bfloat16)
    lifted = lax.dot_general(
        own_restriction, coarse, (((0,), (0,)), ((), ())), preferred_element_type=jnp.float32
    )
    return (accumulated + lifted).astype(jnp.bfloat16)[None, None]


def solution(mesh):
    placed = (
        P("region", "sub", None, None),
        P("region", "sub", None, None),
        P("region", "sub", None, None, None),
        P(None, "region", "sub", None),
        P(),
        P("region", "sub", None, None),
        P("region", "sub", None),
    )
    return jax.shard_map(
        shards,
        mesh=mesh,
        in_specs=placed,
        out_specs=P("region", "sub", None, None),
        check_vma=False,
    )
```

profile of v0, /device:TPU:1, one launch (start us, length us, event | category | flops | bytes accessed | tf_op | source)
XLA Modules:
  0.0 384.2 jit_solution(11332730340993844676)
XLA Ops:
  6.5 1.1 slice_reduce_fusion
  7.7 2.0 copy.96
  9.7 1.2 copy.97
  12.3 10.9 %all-to-all-start = ((bf16[8,64,128]{2,1,0:T(8,128)(2,1)}), bf16[8,64,128]{2,1,0:T(8,128)(2,1)S(1)}, u32[]{:S(2)}, u32[]{:S(2)}) async-start(bf16[8,64,128]{2,1,0:T(8,128)(2,1)} %convert_element_type.77), calls=%async_computation | async-start | bytes 262144 | tf_op jit(solution)/shard_map/all_to_all | solution.py:32
  23.2 7.7 %all-to-all-done = bf16[8,64,128]{2,1,0:T(8,128)(2,1)S(1)} async-done(((bf16[8,64,128]{2,1,0:T(8,128)(2,1)}), bf16[8,64,128]{2,1,0:T(8,128)(2,1)S(1)}, u32[]{:S(2)}, u32[]{:S(2)}) %all-to-all-start) | async-done | bytes 131104 | tf_op jit(solution)/shard_map/all_to_all | solution.py:32
  31.7 12.4 %all-to-all-start.1 = ((bf16[8,64,128]{2,0,1:T(8,128)(2,1)}), bf16[8,64,128]{2,0,1:T(8,128)(2,1)S(1)}, u32[]{:S(2)}, u32[]{:S(2)}) async-start(bf16[8,64,128]{2,0,1:T(8,128)(2,1)} %copy.98), calls=%async_computation.1 | async-start | bytes 262144 | tf_op jit(solution)/shard_map/all_to_all | solution.py:31
  44.1 11.1 %all-to-all-done.1 = bf16[8,64,128]{2,0,1:T(8,128)(2,1)S(1)} async-done(((bf16[8,64,128]{2,0,1:T(8,128)(2,1)}), bf16[8,64,128]{2,0,1:T(8,128)(2,1)S(1)}, u32[]{:S(2)}, u32[]{:S(2)}) %all-to-all-start.1) | async-done | bytes 131104 | tf_op jit(solution)/shard_map/all_to_all | solution.py:31
  55.2 1.3 gather_fusion.1
  56.7 10.7 %all_to_all.80 = bf16[8,64,128]{2,1,0:T(8,128)(2,1)S(1)} all-to-all(bf16[8,64,128]{2,1,0:T(8,128)(2,1)S(1)} %bitcast.164), channel_id=1, replica_groups=mesh['region'=8,'sub'=64] {'region'}, dimensions={0} | all-to-all | bytes 262144 | tf_op jit(solution)/shard_map/all_to_all | solution.py:40
  68.2 5.7 %all-to-all-start.3 = ((bf16[8,64,128]{2,0,1:T(8,128)(2,1)}), bf16[8,64,128]{2,0,1:T(8,128)(2,1)S(1)}, u32[]{:S(2)}, u32[]{:S(2)}) async-start(bf16[8,64,128]{2,0,1:T(8,128)(2,1)} %copy.100), calls=%async_computation.3 | async-start | bytes 262144 | tf_op jit(solution)/shard_map/all_to_all | solution.py:39
  73.9 11.3 %all-to-all-done.3 = bf16[8,64,128]{2,0,1:T(8,128)(2,1)S(1)} async-done(((bf16[8,64,128]{2,0,1:T(8,128)(2,1)}), bf16[8,64,128]{2,0,1:T(8,128)(2,1)S(1)}, u32[]{:S(2)}, u32[]{:S(2)}) %all-to-all-start.3) | async-done | bytes 131104 | tf_op jit(solution)/shard_map/all_to_all | solution.py:39
  85.3 1.1 fusion.30
  86.4 1.3 fusion.12
  87.7 0.9 copy.104
  89.0 1.3 copy.106
  90.3 3.3 bitcast_subtract_fusion.3
  93.6 1.0 copy.135
  94.6 1.6 gather_fusion.2
  97.0 3.4 all-to-all-start.4
  100.4 8.1 %all-to-all-done.4 = bf16[8,64,128]{2,1,0:T(8,128)(2,1)S(1)} async-done(((bf16[8,64,128]{2,1,0:T(8,128)(2,1)}), bf16[8,64,128]{2,1,0:T(8,128)(2,1)S(1)}, u32[]{:S(2)}, u32[]{:S(2)}) %all-to-all-start.4) | async-done | bytes 131104 | tf_op jit(solution)/shard_map/all_to_all | solution.py:32
  108.5 0.7 copy.108
  109.3 5.8 %all-to-all-start.5 = ((bf16[8,64,128]{2,0,1:T(8,128)(2,1)}), bf16[8,64,128]{2,0,1:T(8,128)(2,1)S(1)}, u32[]{:S(2)}, u32[]{:S(2)}) async-start(bf16[8,64,128]{2,0,1:T(8,128)(2,1)} %copy.108), calls=%async_computation.5 | async-start | bytes 262144 | tf_op jit(solution)/shard_map/all_to_all | solution.py:31
  115.1 11.3 %all-to-all-done.5 = bf16[8,64,128]{2,0,1:T(8,128)(2,1)S(1)} async-done(((bf16[8,64,128]{2,0,1:T(8,128)(2,1)}), bf16[8,64,128]{2,0,1:T(8,128)(2,1)S(1)}, u32[]{:S(2)}, u32[]{:S(2)}) %all-to-all-start.5) | async-done | bytes 131104 | tf_op jit(solution)/shard_map/all_to_all | solution.py:31
  126.5 1.3 gather_fusion.3
  127.8 0.8 broadcast_select_fusion.2
  128.6 3.4 all-to-all-start.6
  132.0 8.1 %all-to-all-done.6 = bf16[8,64,128]{2,1,0:T(8,128)(2,1)S(1)} async-done(((bf16[8,64,128]{2,1,0:T(8,128)(2,1)}), bf16[8,64,128]{2,1,0:T(8,128)(2,1)S(1)}, u32[]{:S(2)}, u32[]{:S(2)}) %all-to-all-start.6) | async-done | bytes 131104 | tf_op jit(solution)/shard_map/all_to_all | solution.py:40
  140.1 0.7 copy.110
  140.9 5.8 %all-to-all-start.7 = ((bf16[8,64,128]{2,0,1:T(8,128)(2,1)}), bf16[8,64,128]{2,0,1:T(8,128)(2,1)S(1)}, u32[]{:S(2)}, u32[]{:S(2)}) async-start(bf16[8,64,128]{2,0,1:T(8,128)(2,1)} %copy.110), calls=%async_computation.7 | async-start | bytes 262144 | tf_op jit(solution)/shard_map/all_to_all | solution.py:39
  146.8 11.3 %all-to-all-done.7 = bf16[8,64,128]{2,0,1:T(8,128)(2,1)S(1)} async-done(((bf16[8,64,128]{2,0,1:T(8,128)(2,1)}), bf16[8,64,128]{2,0,1:T(8,128)(2,1)S(1)}, u32[]{:S(2)}, u32[]{:S(2)}) %all-to-all-start.7) | async-done | bytes 131104 | tf_op jit(solution)/shard_map/all_to_all | solution.py:39
  158.1 1.8 fusion.28
  159.9 1.1 copy.129
  161.0 0.8 fusion.40
  161.8 2.3 bitcast_subtract_fusion.2
  164.1 1.4 copy.137
  166.8 3.4 all-to-all-start.8
  170.2 8.1 %all-to-all-done.8 = bf16[8,64,128]{2,1,0:T(8,128)(2,1)S(1)} async-done(((bf16[8,64,128]{2,1,0:T(8,128)(2,1)}), bf16[8,64,128]{2,1,0:T(8,128)(2,1)S(1)}, u32[]{:S(2)}, u32[]{:S(2)}) %all-to-all-start.8) | async-done | bytes 131104 | tf_op jit(solution)/shard_map/all_to_all | solution.py:32
  179.1 5.8 %all-to-all-start.9 = ((bf16[8,64,128]{2,0,1:T(8,128)(2,1)}), bf16[8,64,128]{2,0,1:T(8,128)(2,1)S(1)}, u32[]{:S(2)}, u32[]{:S(2)}) async-start(bf16[8,64,128]{2,0,1:T(8,128)(2,1)} %copy.115), calls=%async_computation.9 | async-start | bytes 262144 | tf_op jit(solution)/shard_map/all_to_all | solution.py:31
  185.0 11.3 %all-to-all-done.9 = bf16[8,64,128]{2,0,1:T(8,128)(2,1)S(1)} async-done(((bf16[8,64,128]{2,0,1:T(8,128)(2,1)}), bf16[8,64,128]{2,0,1:T(8,128)(2,1)S(1)}, u32[]{:S(2)}, u32[]{:S(2)}) %all-to-all-start.9) | async-done | bytes 131104 | tf_op jit(solution)/shard_map/all_to_all | solution.py:31
  196.3 1.3 gather_fusion.5
  197.8 10.7 %all_to_all.81 = bf16[8,64,128]{2,1,0:T(8,128)(2,1)S(1)} all-to-all(bf16[8,64,128]{2,1,0:T(8,128)(2,1)S(1)} %bitcast.165), channel_id=1, replica_groups=mesh['region'=8,'sub'=64] {'region'}, dimensions={0} | all-to-all | bytes 262144 | tf_op jit(solution)/shard_map/all_to_all | solution.py:40
  209.2 5.8 %all-to-all-start.11 = ((bf16[8,64,128]{2,0,1:T(8,128)(2,1)}), bf16[8,64,128]{2,0,1:T(8,128)(2,1)S(1)}, u32[]{:S(2)}, u32[]{:S(2)}) async-start(bf16[8,64,128]{2,0,1:T(8,128)(2,1)} %copy.117), calls=%async_computation.11 | async-start | bytes 262144 | tf_op jit(solution)/shard_map/all_to_all | solution.py:39
  215.0 11.3 %all-to-all-done.11 = bf16[8,64,128]{2,0,1:T(8,128)(2,1)S(1)} async-done(((bf16[8,64,128]{2,0,1:T(8,128)(2,1)}), bf16[8,64,128]{2,0,1:T(8,128)(2,1)S(1)}, u32[]{:S(2)}, u32[]{:S(2)}) %all-to-all-start.11) | async-done | bytes 131104 | tf_op jit(solution)/shard_map/all_to_all | solution.py:39
  226.4 1.1 fusion.26
  227.7 0.8 fusion.38
  228.4 3.4 bitcast_subtract_fusion.1
  231.9 1.0 copy.139
  232.9 1.6 gather_fusion.6
  235.3 3.4 all-to-all-start.12
  238.7 8.1 %all-to-all-done.12 = bf16[8,64,128]{2,1,0:T(8,128)(2,1)S(1)} async-done(((bf16[8,64,128]{2,1,0:T(8,128)(2,1)}), bf16[8,64,128]{2,1,0:T(8,128)(2,1)S(1)}, u32[]{:S(2)}, u32[]{:S(2)}) %all-to-all-start.12) | async-done | bytes 131104 | tf_op jit(solution)/shard_map/all_to_all | solution.py:32
  247.5 5.8 %all-to-all-start.13 = ((bf16[8,64,128]{2,0,1:T(8,128)(2,1)}), bf16[8,64,128]{2,0,1:T(8,128)(2,1)S(1)}, u32[]{:S(2)}, u32[]{:S(2)}) async-start(bf16[8,64,128]{2,0,1:T(8,128)(2,1)} %copy.122), calls=%async_computation.13 | async-start | bytes 262144 | tf_op jit(solution)/shard_map/all_to_all | solution.py:31
  253.5 11.2 %all-to-all-done.13 = bf16[8,64,128]{2,0,1:T(8,128)(2,1)S(1)} async-done(((bf16[8,64,128]{2,0,1:T(8,128)(2,1)}), bf16[8,64,128]{2,0,1:T(8,128)(2,1)S(1)}, u32[]{:S(2)}, u32[]{:S(2)}) %all-to-all-start.13) | async-done | bytes 131104 | tf_op jit(solution)/shard_map/all_to_all | solution.py:31
  264.7 1.3 gather_fusion.7
  266.2 10.7 %all_to_all.82 = bf16[8,64,128]{2,1,0:T(8,128)(2,1)S(1)} all-to-all(bf16[8,64,128]{2,1,0:T(8,128)(2,1)S(1)} %bitcast.166), channel_id=1, replica_groups=mesh['region'=8,'sub'=64] {'region'}, dimensions={0} | all-to-all | bytes 262144 | tf_op jit(solution)/shard_map/all_to_all | solution.py:40
  277.0 16.3 %all_to_all.83 = bf16[8,64,128]{2,0,1:T(8,128)(2,1)S(1)} all-to-all(bf16[8,64,128]{2,0,1:T(8,128)(2,1)S(1)} %copy.124), channel_id=1, replica_groups=mesh['region'=8,'sub'=64] {'sub'}, dimensions={1} | all-to-all | bytes 262144 | tf_op jit(solution)/shard_map/all_to_all | solution.py:39
  293.3 1.8 fusion.24
  295.1 1.1 copy.133
  296.2 0.8 fusion.36
  297.0 0.8 fusion
  297.8 1.0 copy-done.1
  298.8 1.1 fusion.10
  299.9 72.5 %all-gather.2.cloned.1.call-done = bf16[4096,256]{1,0:T(8,128)(2,1)} async-done(((bf16[64,256]{1,0:T(8,128)(2,1)}), bf16[4096,256]{1,0:T(8,128)(2,1)}) %all-gather.2.cloned.1.call-update) | async-done | bytes 2097168 | tf_op jit(solution)/shard_map/all_gather | solution.py:74
  372.4 4.0 %fusion.9 = bf16[1,1,1024,256]{2,3,1,0:T(8,128)(2,1)S(1)} fusion(f32[256,1024]{1,0:T(8,128)} %copy-done.1, f32[256,1024]{1,0:T(8,128)} %get-tuple-element.22, f32[256,1024]{1,0:T(8,128)} %get-tuple-element.18, f32[256,1024]{1,0:T(8,128)} %get-tuple-element.20, bf16[4096,256]{1,0:T(8,128)(2,1)} %all-gather.2.cloned.1.call-done, ...), kind=kOutput, calls=%fused_computation.18 | convolution fusion | flops 169099264 | bytes 7471104 | tf_op jit(solution)/shard_map/dot_general | solution.py:77
  376.4 1.0 copy.128
  (63 shorter events, 9.5 us)
Async XLA Ops:
  6.5 83.8 %copy-start = (bf16[1,1,1024,1024]{3,2,1,0:T(8,128)(2,1)S(1)}, bf16[1,1,1024,1024]{3,2,1,0:T(8,128)(2,1)}, u32[]{:S(2)}) copy-start(bf16[1,1,1024,1024]{3,2,1,0:T(8,128)(2,1)} %param.12) | copy-start | bytes 6291460
  6.5 16.7 %copy-start.3 = (s32[4,512]{1,0:T(4,128)S(1)}, s32[4,512]{1,0:T(4,128)}, u32[]{:S(2)}) copy-start(s32[4,512]{1,0:T(4,128)} %param.15) | copy-start | bytes 24580
  12.3 18.6 %all-to-all-start = ((bf16[8,64,128]{2,1,0:T(8,128)(2,1)}), bf16[8,64,128]{2,1,0:T(8,128)(2,1)S(1)}, u32[]{:S(2)}, u32[]{:S(2)}) async-start(bf16[8,64,128]{2,1,0:T(8,128)(2,1)} %convert_element_type.77), calls=%async_computation | async-start | bytes 262144 | tf_op jit(solution)/shard_map/all_to_all | solution.py:32
  31.7 23.5 %all-to-all-start.1 = ((bf16[8,64,128]{2,0,1:T(8,128)(2,1)}), bf16[8,64,128]{2,0,1:T(8,128)(2,1)S(1)}, u32[]{:S(2)}, u32[]{:S(2)}) async-start(bf16[8,64,128]{2,0,1:T(8,128)(2,1)} %copy.98), calls=%async_computation.1 | async-start | bytes 262144 | tf_op jit(solution)/shard_map/all_to_all | solution.py:31
  68.2 17.1 %all-to-all-start.3 = ((bf16[8,64,128]{2,0,1:T(8,128)(2,1)}), bf16[8,64,128]{2,0,1:T(8,128)(2,1)S(1)}, u32[]{:S(2)}, u32[]{:S(2)}) async-start(bf16[8,64,128]{2,0,1:T(8,128)(2,1)} %copy.100), calls=%async_computation.3 | async-start | bytes 262144 | tf_op jit(solution)/shard_map/all_to_all | solution.py:39
  97.0 11.5 %all-to-all-start.4 = ((bf16[8,64,128]{2,1,0:T(8,128)(2,1)}), bf16[8,64,128]{2,1,0:T(8,128)(2,1)S(1)}, u32[]{:S(2)}, u32[]{:S(2)}) async-start(bf16[8,64,128]{2,1,0:T(8,128)(2,1)} %convert_element_type.83), calls=%async_computation.4 | async-start | bytes 262144 | tf_op jit(solution)/shard_map/all_to_all | solution.py:32
  109.3 17.2 %all-to-all-start.5 = ((bf16[8,64,128]{2,0,1:T(8,128)(2,1)}), bf16[8,64,128]{2,0,1:T(8,128)(2,1)S(1)}, u32[]{:S(2)}, u32[]{:S(2)}) async-start(bf16[8,64,128]{2,0,1:T(8,128)(2,1)} %copy.108), calls=%async_computation.5 | async-start | bytes 262144 | tf_op jit(solution)/shard_map/all_to_all | solution.py:31
  128.6 11.5 %all-to-all-start.6 = ((bf16[8,64,128]{2,1,0:T(8,128)(2,1)}), bf16[8,64,128]{2,1,0:T(8,128)(2,1)S(1)}, u32[]{:S(2)}, u32[]{:S(2)}) async-start(bf16[8,64,128]{2,1,0:T(8,128)(2,1)} %bitcast.17), calls=%async_computation.6 | async-start | bytes 262144 | tf_op jit(solution)/shard_map/all_to_all | solution.py:40
  140.9 17.2 %all-to-all-start.7 = ((bf16[8,64,128]{2,0,1:T(8,128)(2,1)}), bf16[8,64,128]{2,0,1:T(8,128)(2,1)S(1)}, u32[]{:S(2)}, u32[]{:S(2)}) async-start(bf16[8,64,128]{2,0,1:T(8,128)(2,1)} %copy.110), calls=%async_computation.7 | async-start | bytes 262144 | tf_op jit(solution)/shard_map/all_to_all | solution.py:39
  166.8 11.5 %all-to-all-start.8 = ((bf16[8,64,128]{2,1,0:T(8,128)(2,1)}), bf16[8,64,128]{2,1,0:T(8,128)(2,1)S(1)}, u32[]{:S(2)}, u32[]{:S(2)}) async-start(bf16[8,64,128]{2,1,0:T(8,128)(2,1)} %convert_element_type.86), calls=%async_computation.8 | async-start | bytes 262144 | tf_op jit(solution)/shard_map/all_to_all | solution.py:32
  179.1 17.2 %all-to-all-start.9 = ((bf16[8,64,128]{2,0,1:T(8,128)(2,1)}), bf16[8,64,128]{2,0,1:T(8,128)(2,1)S(1)}, u32[]{:S(2)}, u32[]{:S(2)}) async-start(bf16[8,64,128]{2,0,1:T(8,128)(2,1)} %copy.115), calls=%async_computation.9 | async-start | bytes 262144 | tf_op jit(solution)/shard_map/all_to_all | solution.py:31
  209.2 17.1 %all-to-all-start.11 = ((bf16[8,64,128]{2,0,1:T(8,128)(2,1)}), bf16[8,64,128]{2,0,1:T(8,128)(2,1)S(1)}, u32[]{:S(2)}, u32[]{:S(2)}) async-start(bf16[8,64,128]{2,0,1:T(8,128)(2,1)} %copy.117), calls=%async_computation.11 | async-start | bytes 262144 | tf_op jit(solution)/shard_map/all_to_all | solution.py:39
  235.3 11.5 %all-to-all-start.12 = ((bf16[8,64,128]{2,1,0:T(8,128)(2,1)}), bf16[8,64,128]{2,1,0:T(8,128)(2,1)S(1)}, u32[]{:S(2)}, u32[]{:S(2)}) async-start(bf16[8,64,128]{2,1,0:T(8,128)(2,1)} %convert_element_type.89), calls=%async_computation.12 | async-start | bytes 262144 | tf_op jit(solution)/shard_map/all_to_all | solution.py:32
  247.5 17.2 %all-to-all-start.13 = ((bf16[8,64,128]{2,0,1:T(8,128)(2,1)}), bf16[8,64,128]{2,0,1:T(8,128)(2,1)S(1)}, u32[]{:S(2)}, u32[]{:S(2)}) async-start(bf16[8,64,128]{2,0,1:T(8,128)(2,1)} %copy.122), calls=%async_computation.13 | async-start | bytes 262144 | tf_op jit(solution)/shard_map/all_to_all | solution.py:31
  253.4 119.0 %all-gather.2.cloned.1.call-start = ((), (), s32[]{:S(2)}) async-start(), calls=%async_computation.16 | async-start | bytes 2129920 | tf_op jit(solution)/shard_map/all_gather | solution.py:74
  297.0 1.8 copy-start.2
  297.8 1.0 copy-start.1
Sparse Core Ops, SparseCore 0:
  300.1 72.3 all-gather.1
where the time goes:
time: 386 us; the launch traced here: 384 us
  waiting for transfers between devices  192 us (50%)
  starting transfers between devices  71.6 us (19%)
  blocking collectives  48.4 us (13%)
  local copies, waits for them, and re-layouts  32.8 us (8%)
  matrix products  24.2 us (6%)
  between operations  13.9 us (4%)
    all_gather x1, waiting for transfers between devices, shards(): lax.all_gather(projected, 'sub', axis=0, tiled=True)  72.5 us
    all_to_all x4, waiting for transfers between devices, shards(): lax.all_to_all(lax.all_to_all(pieces, 'region', split_axis=0, concat_axis...  44.9 us
    all_to_all x3, waiting for transfers between devices, shards(): lax.all_to_all(lax.all_to_all(relayed.reshape(region_peers, sub_peers, pi...  33.9 us
    all_to_all x4, waiting for transfers between devices, shards(): lax.all_to_all(pieces, 'region', split_axis=0, concat_axis=0, tiled=True)  32.1 us
    all_to_all x3, blocking collectives, shards(): lax.all_to_all(relayed.reshape(region_peers, sub_peers, piece_len), 'regi...  32.1 us
    all_to_all x4, starting transfers between devices, shards(): lax.all_to_all(lax.all_to_all(pieces, 'region', split_axis=0, concat_axis...  29.9 us
    all_to_all x4, starting transfers between devices, shards(): lax.all_to_all(pieces, 'region', split_axis=0, concat_axis=0, tiled=True)  21 us
    all_to_all x3, starting transfers between devices, shards(): lax.all_to_all(lax.all_to_all(relayed.reshape(region_peers, sub_peers, pi...  17.3 us
  transfers between devices with their start and end apart: 13, of which 13 were waited for; matrix products, arithmetic and copies ran while one was open for 0% of the time, Pallas kernels for 0%

commit v1 on v0

--- a/solution.py
+++ b/solution.py
@@ -71,7 +71,9 @@
     own_rows = coarse_rows[0]
     coarse = jnp.dot(
         own_rows,
-        lax.all_gather(projected, "sub", axis=0, tiled=True),
+        jnp.concatenate(
+            lax.all_to_all(jnp.stack([projected] * lax.axis_size("sub")), "sub", 0, 0), axis=0
+        ),
         preferred_element_type=jnp.float32,
     ).astype(jnp.bfloat16)
     lifted = lax.dot_general(

time: 386 us -> 355 us (0.920)
  waiting for transfers between devices: 192 us -> 119 us
  blocking collectives: 48.4 us -> 103 us
  between operations: 13.9 us -> 0.53 us
    all_gather x1 -> x0, waiting for transfers between devices: 72.5 us -> none  [shards(): lax.all_gather(projected, 'sub', axis=0, tiled=True)]
    all_to_all x0 -> x1, blocking collectives: none -> 54.4 us  [shards(): lax.all_to_all(jnp.stack([projected] * lax.axis_size('sub')), 'sub', 0, 0)]
  transfers between devices with their start and end apart: 13 -> 12, of which waited for: 13 -> 12; matrix products, arithmetic and copies ran while one was open for 0% -> 0% of each run, Pallas kernels for 0% -> 0%
where the time goes in v1:
time: 355 us; the launch traced here: 353 us
  waiting for transfers between devices  119 us (34%)
  blocking collectives  103 us (29%)
  starting transfers between devices  71.6 us (20%)
  local copies, waits for them, and re-layouts  33.5 us (9%)
  matrix products  24.1 us (7%)
    all_to_all x1, blocking collectives, shards(): lax.all_to_all(jnp.stack([projected] * lax.axis_size('sub')), 'sub', 0, 0)  54.4 us
    all_to_all x4, waiting for transfers between devices, shards(): lax.all_to_all(lax.all_to_all(pieces, 'region', split_axis=0, concat_axis...  45 us
    all_to_all x3, waiting for transfers between devices, shards(): lax.all_to_all(lax.all_to_all(relayed.reshape(region_peers, sub_peers, pi...  33.9 us
    all_to_all x4, waiting for transfers between devices, shards(): lax.all_to_all(pieces, 'region', split_axis=0, concat_axis=0, tiled=True)  32.1 us
    all_to_all x3, blocking collectives, shards(): lax.all_to_all(relayed.reshape(region_peers, sub_peers, piece_len), 'regi...  32.1 us
    all_to_all x4, starting transfers between devices, shards(): lax.all_to_all(lax.all_to_all(pieces, 'region', split_axis=0, concat_axis...  29.9 us
    all_to_all x4, starting transfers between devices, shards(): lax.all_to_all(pieces, 'region', split_axis=0, concat_axis=0, tiled=True)  21 us
    all_to_all x3, starting transfers between devices, shards(): lax.all_to_all(lax.all_to_all(relayed.reshape(region_peers, sub_peers, pi...  17.3 us
  transfers between devices with their start and end apart: 12, of which 12 were waited for; matrix products, arithmetic and copies ran while one was open for 0% of the time, Pallas kernels for 0%

profile of v1, /device:TPU:1, one launch (start us, length us, event | category | flops | bytes accessed | tf_op | source)
XLA Modules:
  0.0 353.4 jit_solution(14177012602061867764)
XLA Ops:
  0.0 1.1 slice_reduce_fusion
  1.2 2.0 copy.96
  3.2 1.2 copy.97
  5.8 10.9 %all-to-all-start = ((bf16[8,64,128]{2,1,0:T(8,128)(2,1)}), bf16[8,64,128]{2,1,0:T(8,128)(2,1)S(1)}, u32[]{:S(2)}, u32[]{:S(2)}) async-start(bf16[8,64,128]{2,1,0:T(8,128)(2,1)} %convert_element_type.77), calls=%async_computation | async-start | bytes 262144 | tf_op jit(solution)/shard_map/all_to_all | solution.py:32
  16.7 7.7 %all-to-all-done = bf16[8,64,128]{2,1,0:T(8,128)(2,1)S(1)} async-done(((bf16[8,64,128]{2,1,0:T(8,128)(2,1)}), bf16[8,64,128]{2,1,0:T(8,128)(2,1)S(1)}, u32[]{:S(2)}, u32[]{:S(2)}) %all-to-all-start) | async-done | bytes 131104 | tf_op jit(solution)/shard_map/all_to_all | solution.py:32
  25.1 12.4 %all-to-all-start.1 = ((bf16[8,64,128]{2,0,1:T(8,128)(2,1)}), bf16[8,64,128]{2,0,1:T(8,128)(2,1)S(1)}, u32[]{:S(2)}, u32[]{:S(2)}) async-start(bf16[8,64,128]{2,0,1:T(8,128)(2,1)} %copy.98), calls=%async_computation.1 | async-start | bytes 262144 | tf_op jit(solution)/shard_map/all_to_all | solution.py:31
  37.6 11.1 %all-to-all-done.1 = bf16[8,64,128]{2,0,1:T(8,128)(2,1)S(1)} async-done(((bf16[8,64,128]{2,0,1:T(8,128)(2,1)}), bf16[8,64,128]{2,0,1:T(8,128)(2,1)S(1)}, u32[]{:S(2)}, u32[]{:S(2)}) %all-to-all-start.1) | async-done | bytes 131104 | tf_op jit(solution)/shard_map/all_to_all | solution.py:31
  48.7 1.3 gather_fusion.1
  50.2 10.7 %all_to_all.85 = bf16[8,64,128]{2,1,0:T(8,128)(2,1)S(1)} all-to-all(bf16[8,64,128]{2,1,0:T(8,128)(2,1)S(1)} %bitcast.166), channel_id=1, replica_groups=mesh['region'=8,'sub'=64] {'region'}, dimensions={0} | all-to-all | bytes 262144 | tf_op jit(solution)/shard_map/all_to_all | solution.py:40
  61.6 5.7 %all-to-all-start.3 = ((bf16[8,64,128]{2,0,1:T(8,128)(2,1)}), bf16[8,64,128]{2,0,1:T(8,128)(2,1)S(1)}, u32[]{:S(2)}, u32[]{:S(2)}) async-start(bf16[8,64,128]{2,0,1:T(8,128)(2,1)} %copy.100), calls=%async_computation.3 | async-start | bytes 262144 | tf_op jit(solution)/shard_map/all_to_all | solution.py:39
  67.4 11.3 %all-to-all-done.3 = bf16[8,64,128]{2,0,1:T(8,128)(2,1)S(1)} async-done(((bf16[8,64,128]{2,0,1:T(8,128)(2,1)}), bf16[8,64,128]{2,0,1:T(8,128)(2,1)S(1)}, u32[]{:S(2)}, u32[]{:S(2)}) %all-to-all-start.3) | async-done | bytes 131104 | tf_op jit(solution)/shard_map/all_to_all | solution.py:39
  78.8 1.1 fusion.30
  79.9 1.3 fusion.12
  81.2 0.9 copy.104
  82.5 1.3 copy.106
  83.8 3.3 bitcast_subtract_fusion.3
  87.1 1.0 copy.135
  88.1 1.6 gather_fusion.2
  90.5 3.4 all-to-all-start.4
  93.8 8.1 %all-to-all-done.4 = bf16[8,64,128]{2,1,0:T(8,128)(2,1)S(1)} async-done(((bf16[8,64,128]{2,1,0:T(8,128)(2,1)}), bf16[8,64,128]{2,1,0:T(8,128)(2,1)S(1)}, u32[]{:S(2)}, u32[]{:S(2)}) %all-to-all-start.4) | async-done | bytes 131104 | tf_op jit(solution)/shard_map/all_to_all | solution.py:32
  102.0 0.7 copy.108
  102.7 5.8 %all-to-all-start.5 = ((bf16[8,64,128]{2,0,1:T(8,128)(2,1)}), bf16[8,64,128]{2,0,1:T(8,128)(2,1)S(1)}, u32[]{:S(2)}, u32[]{:S(2)}) async-start(bf16[8,64,128]{2,0,1:T(8,128)(2,1)} %copy.108), calls=%async_computation.5 | async-start | bytes 262144 | tf_op jit(solution)/shard_map/all_to_all | solution.py:31
  108.6 11.3 %all-to-all-done.5 = bf16[8,64,128]{2,0,1:T(8,128)(2,1)S(1)} async-done(((bf16[8,64,128]{2,0,1:T(8,128)(2,1)}), bf16[8,64,128]{2,0,1:T(8,128)(2,1)S(1)}, u32[]{:S(2)}, u32[]{:S(2)}) %all-to-all-start.5) | async-done | bytes 131104 | tf_op jit(solution)/shard_map/all_to_all | solution.py:31
  119.9 1.3 gather_fusion.3
  121.3 0.8 broadcast_select_fusion.2
  122.1 3.4 all-to-all-start.6
  125.5 8.1 %all-to-all-done.6 = bf16[8,64,128]{2,1,0:T(8,128)(2,1)S(1)} async-done(((bf16[8,64,128]{2,1,0:T(8,128)(2,1)}), bf16[8,64,128]{2,1,0:T(8,128)(2,1)S(1)}, u32[]{:S(2)}, u32[]{:S(2)}) %all-to-all-start.6) | async-done | bytes 131104 | tf_op jit(solution)/shard_map/all_to_all | solution.py:40
  133.6 0.7 copy.110
  134.3 5.8 %all-to-all-start.7 = ((bf16[8,64,128]{2,0,1:T(8,128)(2,1)}), bf16[8,64,128]{2,0,1:T(8,128)(2,1)S(1)}, u32[]{:S(2)}, u32[]{:S(2)}) async-start(bf16[8,64,128]{2,0,1:T(8,128)(2,1)} %copy.110), calls=%async_computation.7 | async-start | bytes 262144 | tf_op jit(solution)/shard_map/all_to_all | solution.py:39
  140.2 11.3 %all-to-all-done.7 = bf16[8,64,128]{2,0,1:T(8,128)(2,1)S(1)} async-done(((bf16[8,64,128]{2,0,1:T(8,128)(2,1)}), bf16[8,64,128]{2,0,1:T(8,128)(2,1)S(1)}, u32[]{:S(2)}, u32[]{:S(2)}) %all-to-all-start.7) | async-done | bytes 131104 | tf_op jit(solution)/shard_map/all_to_all | solution.py:39
  151.6 1.8 fusion.28
  153.4 1.1 copy.129
  154.5 0.8 fusion.40
  155.3 2.3 bitcast_subtract_fusion.2
  157.5 1.4 copy.137
  160.3 3.4 all-to-all-start.8
  163.7 8.1 %all-to-all-done.8 = bf16[8,64,128]{2,1,0:T(8,128)(2,1)S(1)} async-done(((bf16[8,64,128]{2,1,0:T(8,128)(2,1)}), bf16[8,64,128]{2,1,0:T(8,128)(2,1)S(1)}, u32[]{:S(2)}, u32[]{:S(2)}) %all-to-all-start.8) | async-done | bytes 131104 | tf_op jit(solution)/shard_map/all_to_all | solution.py:32
  171.8 0.7 copy.115
  172.6 5.8 %all-to-all-start.9 = ((bf16[8,64,128]{2,0,1:T(8,128)(2,1)}), bf16[8,64,128]{2,0,1:T(8,128)(2,1)S(1)}, u32[]{:S(2)}, u32[]{:S(2)}) async-start(bf16[8,64,128]{2,0,1:T(8,128)(2,1)} %copy.115), calls=%async_computation.9 | async-start | bytes 262144 | tf_op jit(solution)/shard_map/all_to_all | solution.py:31
  178.5 11.3 %all-to-all-done.9 = bf16[8,64,128]{2,0,1:T(8,128)(2,1)S(1)} async-done(((bf16[8,64,128]{2,0,1:T(8,128)(2,1)}), bf16[8,64,128]{2,0,1:T(8,128)(2,1)S(1)}, u32[]{:S(2)}, u32[]{:S(2)}) %all-to-all-start.9) | async-done | bytes 131104 | tf_op jit(solution)/shard_map/all_to_all | solution.py:31
  189.8 1.3 gather_fusion.5
  191.3 10.7 %all_to_all.86 = bf16[8,64,128]{2,1,0:T(8,128)(2,1)S(1)} all-to-all(bf16[8,64,128]{2,1,0:T(8,128)(2,1)S(1)} %bitcast.167), channel_id=1, replica_groups=mesh['region'=8,'sub'=64] {'region'}, dimensions={0} | all-to-all | bytes 262144 | tf_op jit(solution)/shard_map/all_to_all | solution.py:40
  202.0 0.7 copy.117
  202.7 5.8 %all-to-all-start.11 = ((bf16[8,64,128]{2,0,1:T(8,128)(2,1)}), bf16[8,64,128]{2,0,1:T(8,128)(2,1)S(1)}, u32[]{:S(2)}, u32[]{:S(2)}) async-start(bf16[8,64,128]{2,0,1:T(8,128)(2,1)} %copy.117), calls=%async_computation.11 | async-start | bytes 262144 | tf_op jit(solution)/shard_map/all_to_all | solution.py:39
  208.5 11.3 %all-to-all-done.11 = bf16[8,64,128]{2,0,1:T(8,128)(2,1)S(1)} async-done(((bf16[8,64,128]{2,0,1:T(8,128)(2,1)}), bf16[8,64,128]{2,0,1:T(8,128)(2,1)S(1)}, u32[]{:S(2)}, u32[]{:S(2)}) %all-to-all-start.11) | async-done | bytes 131104 | tf_op jit(solution)/shard_map/all_to_all | solution.py:39
  219.9 1.1 fusion.26
  221.1 0.8 fusion.38
  221.9 3.5 bitcast_subtract_fusion.1
  225.4 1.0 copy.139
  226.4 1.6 gather_fusion.6
  228.8 3.4 all-to-all-start.12
  232.2 8.1 %all-to-all-done.12 = bf16[8,64,128]{2,1,0:T(8,128)(2,1)S(1)} async-done(((bf16[8,64,128]{2,1,0:T(8,128)(2,1)}), bf16[8,64,128]{2,1,0:T(8,128)(2,1)S(1)}, u32[]{:S(2)}, u32[]{:S(2)}) %all-to-all-start.12) | async-done | bytes 131104 | tf_op jit(solution)/shard_map/all_to_all | solution.py:32
  241.0 5.8 %all-to-all-start.13 = ((bf16[8,64,128]{2,0,1:T(8,128)(2,1)}), bf16[8,64,128]{2,0,1:T(8,128)(2,1)S(1)}, u32[]{:S(2)}, u32[]{:S(2)}) async-start(bf16[8,64,128]{2,0,1:T(8,128)(2,1)} %copy.122), calls=%async_computation.13 | async-start | bytes 262144 | tf_op jit(solution)/shard_map/all_to_all | solution.py:31
  246.9 11.3 %all-to-all-done.13 = bf16[8,64,128]{2,0,1:T(8,128)(2,1)S(1)} async-done(((bf16[8,64,128]{2,0,1:T(8,128)(2,1)}), bf16[8,64,128]{2,0,1:T(8,128)(2,1)S(1)}, u32[]{:S(2)}, u32[]{:S(2)}) %all-to-all-start.13) | async-done | bytes 131104 | tf_op jit(solution)/shard_map/all_to_all | solution.py:31
  258.2 1.3 gather_fusion.7
  259.7 10.7 %all_to_all.87 = bf16[8,64,128]{2,1,0:T(8,128)(2,1)S(1)} all-to-all(bf16[8,64,128]{2,1,0:T(8,128)(2,1)S(1)} %bitcast.168), channel_id=1, replica_groups=mesh['region'=8,'sub'=64] {'region'}, dimensions={0} | all-to-all | bytes 262144 | tf_op jit(solution)/shard_map/all_to_all | solution.py:40
  270.5 16.3 %all_to_all.88 = bf16[8,64,128]{2,0,1:T(8,128)(2,1)S(1)} all-to-all(bf16[8,64,128]{2,0,1:T(8,128)(2,1)S(1)} %copy.124), channel_id=1, replica_groups=mesh['region'=8,'sub'=64] {'sub'}, dimensions={1} | all-to-all | bytes 262144 | tf_op jit(solution)/shard_map/all_to_all | solution.py:39
  286.9 1.8 fusion.24
  288.7 1.1 copy.133
  289.8 0.8 fusion.36
  290.5 0.8 fusion
  292.4 54.4 %all_to_all.89 = bf16[64,64,256]{2,1,0:T(8,128)(2,1)} all-to-all(bf16[64,64,256]{2,1,0:T(8,128)(2,1)S(1)} %stack.2), channel_id=1, replica_groups=mesh['region'=8,'sub'=64] {'sub'}, dimensions={0} | all-to-all | bytes 4194304 | tf_op jit(solution)/shard_map/all_to_all | solution.py:75
  346.9 4.5 %fusion.9 = bf16[1,1,1024,256]{2,3,1,0:T(8,128)(2,1)} fusion(f32[256,1024]{1,0:T(8,128)} %copy-done.1, f32[256,1024]{1,0:T(8,128)} %get-tuple-element.22, f32[256,1024]{1,0:T(8,128)S(1)} %copy-done.2, f32[256,1024]{1,0:T(8,128)} %get-tuple-element.20, bf16[4096,256]{1,0:T(8,128)(2,1)} %bitcast.152, bf16[1,64,4096]{2,1,0:T(8,128)(2,1)} %param.17, ...), kind=kOutput, calls=%fused_computation.18 | convolution fusion | flops 169099264 | bytes 7471104 | tf_op jit(solution)/shard_map/dot_general | solution.py:79
  351.4 2.0 copy.128
  (64 shorter events, 9.1 us)
Async XLA Ops:
  0.0 83.8 %copy-start = (bf16[1,1,1024,1024]{3,2,1,0:T(8,128)(2,1)S(1)}, bf16[1,1,1024,1024]{3,2,1,0:T(8,128)(2,1)}, u32[]{:S(2)}) copy-start(bf16[1,1,1024,1024]{3,2,1,0:T(8,128)(2,1)} %param.12) | copy-start | bytes 6291460
  0.0 16.7 %copy-start.4 = (s32[4,512]{1,0:T(4,128)S(1)}, s32[4,512]{1,0:T(4,128)}, u32[]{:S(2)}) copy-start(s32[4,512]{1,0:T(4,128)} %param.15) | copy-start | bytes 24580
  5.8 18.6 %all-to-all-start = ((bf16[8,64,128]{2,1,0:T(8,128)(2,1)}), bf16[8,64,128]{2,1,0:T(8,128)(2,1)S(1)}, u32[]{:S(2)}, u32[]{:S(2)}) async-start(bf16[8,64,128]{2,1,0:T(8,128)(2,1)} %convert_element_type.77), calls=%async_computation | async-start | bytes 262144 | tf_op jit(solution)/shard_map/all_to_all | solution.py:32
  25.1 23.5 %all-to-all-start.1 = ((bf16[8,64,128]{2,0,1:T(8,128)(2,1)}), bf16[8,64,128]{2,0,1:T(8,128)(2,1)S(1)}, u32[]{:S(2)}, u32[]{:S(2)}) async-start(bf16[8,64,128]{2,0,1:T(8,128)(2,1)} %copy.98), calls=%async_computation.1 | async-start | bytes 262144 | tf_op jit(solution)/shard_map/all_to_all | solution.py:31
  61.6 17.1 %all-to-all-start.3 = ((bf16[8,64,128]{2,0,1:T(8,128)(2,1)}), bf16[8,64,128]{2,0,1:T(8,128)(2,1)S(1)}, u32[]{:S(2)}, u32[]{:S(2)}) async-start(bf16[8,64,128]{2,0,1:T(8,128)(2,1)} %copy.100), calls=%async_computation.3 | async-start | bytes 262144 | tf_op jit(solution)/shard_map/all_to_all | solution.py:39
  90.5 11.5 %all-to-all-start.4 = ((bf16[8,64,128]{2,1,0:T(8,128)(2,1)}), bf16[8,64,128]{2,1,0:T(8,128)(2,1)S(1)}, u32[]{:S(2)}, u32[]{:S(2)}) async-start(bf16[8,64,128]{2,1,0:T(8,128)(2,1)} %convert_element_type.83), calls=%async_computation.4 | async-start | bytes 262144 | tf_op jit(solution)/shard_map/all_to_all | solution.py:32
  102.7 17.2 %all-to-all-start.5 = ((bf16[8,64,128]{2,0,1:T(8,128)(2,1)}), bf16[8,64,128]{2,0,1:T(8,128)(2,1)S(1)}, u32[]{:S(2)}, u32[]{:S(2)}) async-start(bf16[8,64,128]{2,0,1:T(8,128)(2,1)} %copy.108), calls=%async_computation.5 | async-start | bytes 262144 | tf_op jit(solution)/shard_map/all_to_all | solution.py:31
  122.1 11.5 %all-to-all-start.6 = ((bf16[8,64,128]{2,1,0:T(8,128)(2,1)}), bf16[8,64,128]{2,1,0:T(8,128)(2,1)S(1)}, u32[]{:S(2)}, u32[]{:S(2)}) async-start(bf16[8,64,128]{2,1,0:T(8,128)(2,1)} %bitcast.17), calls=%async_computation.6 | async-start | bytes 262144 | tf_op jit(solution)/shard_map/all_to_all | solution.py:40
  134.3 17.2 %all-to-all-start.7 = ((bf16[8,64,128]{2,0,1:T(8,128)(2,1)}), bf16[8,64,128]{2,0,1:T(8,128)(2,1)S(1)}, u32[]{:S(2)}, u32[]{:S(2)}) async-start(bf16[8,64,128]{2,0,1:T(8,128)(2,1)} %copy.110), calls=%async_computation.7 | async-start | bytes 262144 | tf_op jit(solution)/shard_map/all_to_all | solution.py:39
  160.3 11.5 %all-to-all-start.8 = ((bf16[8,64,128]{2,1,0:T(8,128)(2,1)}), bf16[8,64,128]{2,1,0:T(8,128)(2,1)S(1)}, u32[]{:S(2)}, u32[]{:S(2)}) async-start(bf16[8,64,128]{2,1,0:T(8,128)(2,1)} %convert_element_type.86), calls=%async_computation.8 | async-start | bytes 262144 | tf_op jit(solution)/shard_map/all_to_all | solution.py:32
  172.6 17.2 %all-to-all-start.9 = ((bf16[8,64,128]{2,0,1:T(8,128)(2,1)}), bf16[8,64,128]{2,0,1:T(8,128)(2,1)S(1)}, u32[]{:S(2)}, u32[]{:S(2)}) async-start(bf16[8,64,128]{2,0,1:T(8,128)(2,1)} %copy.115), calls=%async_computation.9 | async-start | bytes 262144 | tf_op jit(solution)/shard_map/all_to_all | solution.py:31
  202.7 17.1 %all-to-all-start.11 = ((bf16[8,64,128]{2,0,1:T(8,128)(2,1)}), bf16[8,64,128]{2,0,1:T(8,128)(2,1)S(1)}, u32[]{:S(2)}, u32[]{:S(2)}) async-start(bf16[8,64,128]{2,0,1:T(8,128)(2,1)} %copy.117), calls=%async_computation.11 | async-start | bytes 262144 | tf_op jit(solution)/shard_map/all_to_all | solution.py:39
  228.8 11.5 %all-to-all-start.12 = ((bf16[8,64,128]{2,1,0:T(8,128)(2,1)}), bf16[8,64,128]{2,1,0:T(8,128)(2,1)S(1)}, u32[]{:S(2)}, u32[]{:S(2)}) async-start(bf16[8,64,128]{2,1,0:T(8,128)(2,1)} %convert_element_type.89), calls=%async_computation.12 | async-start | bytes 262144 | tf_op jit(solution)/shard_map/all_to_all | solution.py:32
  241.0 17.2 %all-to-all-start.13 = ((bf16[8,64,128]{2,0,1:T(8,128)(2,1)}), bf16[8,64,128]{2,0,1:T(8,128)(2,1)S(1)}, u32[]{:S(2)}, u32[]{:S(2)}) async-start(bf16[8,64,128]{2,0,1:T(8,128)(2,1)} %copy.122), calls=%async_computation.13 | async-start | bytes 262144 | tf_op jit(solution)/shard_map/all_to_all | solution.py:31
  290.5 0.9 copy-start.3
  291.4 1.0 copy-start.1
  292.4 54.5 %copy-start.2 = (f32[256,1024]{1,0:T(8,128)S(1)}, f32[256,1024]{1,0:T(8,128)}, u32[]{:S(2)}) copy-start(f32[256,1024]{1,0:T(8,128)} %get-tuple-element.18) | copy-start | bytes 3145732
